TPU v7x, 256 devices: a whole 4x4x8 slice. The times are simulated.
256 devices in a mesh: dp: 32 (over x, z_lo, core), fsdp: 8 (over y, z_hi).
Axes of the slice: x: 4, y: 4, z: 8 (z_hi: 2, z_lo: 4; z = z_hi * 4 + z_lo), core: 2. Of those that a mesh axis runs over, the one named last changes fastest.
Arguments:
- stream_rows: bfloat16 [16384, 4096], P(('dp', 'fsdp')), may hold values from -6 to 6
- ln_gain: float32 [4096], replicated, may hold values from 0.1 to 1.9
- ln_bias: float32 [4096], replicated, may hold values from -2 to 2
- w_q: bfloat16 [4096, 2048], P(None, 'fsdp')
- w_k: bfloat16 [4096, 2048], P(None, 'fsdp')
- w_v: bfloat16 [4096, 2048], P(None, 'fsdp'), may hold values from -0.09375 to 0.09375
- w_o: bfloat16 [2048, 4096], P('fsdp'), may hold values from -0.1875 to 0.1875
- scale_ls: float32 [4096], P('fsdp'), may hold values from 0.5 to 2
- sides: int32 [32, 1], P('dp'), may hold values from 10 to 18, as said below
- offsets: int32 [32, 1], P('dp'), may hold values from 0 to 0, as said below
- owners: int32 [32, 1], replicated, may hold values from 0 to 31, as said below
Outputs:
- delivered: bfloat16 [32, 1, 81, 4, 4096], P('dp', None, None, None, 'fsdp')
Inputs may be any that keep to these rules, and one draw needn't show every extreme that they name: `sides`: every side is even, and some image has side 18 in every draw. `offsets`: within a group the images lie back to back in index order from row 0, each taking 5 + side * side rows; the rows after the last image are padding. owners[g, j] = (g + c_j) mod 32, with offsets c_j that differ between image indices j; so the images of one group have different owners and every owner receives exactly one image of each index j.
All inputs are finite; a program needn't handle non-finite values.
Results may differ from a plain program's by a relative error of at most 0.012.
Values may be sent and summed in bfloat16 or wider, within the bound.
No kernel may reach another device: no remote copies, remote signals or barrier semaphores. Data moves between devices by JAX's collectives and lax.ppermute only.
A program may use at most 128 MiB of HBM per device.

v0:
```python
import math
import jax
import jax.numpy as jnp
from jax import lax
from jax.sharding import PartitionSpec as P

HEAD = 128
EXTRA = 5
CAP = 81
norm_eps = 1e-06


def shifted(array, axis, by):
    count = lax.axis_size(axis)
    return lax.ppermute(array, axis, [(i, (i + by) % count) for i in range(count)])


def layer_norm(raw_rows, ln_gain, ln_bias):
    values = raw_rows.astype(jnp.float32)
    centre = jnp.mean(values, axis=-1, keepdims=True)
    spread = jnp.mean(jnp.square(values - centre), axis=-1, keepdims=True)
    return ((values - centre) * lax.rsqrt(spread + norm_eps) * ln_gain + ln_bias).astype(
        jnp.bfloat16
    )


def row_layout(side_row, offset_row, count):
    row_ids = jnp.arange(count, dtype=jnp.int32)
    lengths = EXTRA + side_row * side_row
    inside = (
        (row_ids[:, None] >= offset_row[None, :])
        & (row_ids[:, None] < (offset_row + lengths)[None, :])
    ).astype(jnp.int32)
    covered = jnp.sum(inside, axis=1)
    image_ids = jnp.arange(side_row.shape[0], dtype=jnp.int32)
    segment = jnp.sum(inside * image_ids[None, :], axis=1) + (1 - covered) * side_row.shape[0]
    first_row = jnp.sum(inside * offset_row[None, :], axis=1)
    side_len = jnp.sum(inside * side_row[None, :], axis=1) + (1 - covered)
    patch_id = row_ids - first_row - EXTRA
    is_patch = (covered == 1) & (patch_id >= 0)
    clipped = jnp.maximum(patch_id, 0)
    across = clipped // side_len
    along = clipped % side_len
    side_float = side_len.astype(jnp.float32)
    coord_one = jnp.where(
        is_patch,
        (2 * across + 1).astype(jnp.float32) / side_float - 1.0,
        jnp.zeros_like(side_float),
    )
    coord_two = jnp.where(
        is_patch, (2 * along + 1).astype(jnp.float32) / side_float - 1.0, jnp.zeros_like(side_float)
    )
    return (segment, coord_one, coord_two)


def rotary_tables(coord_one, coord_two, head_size):
    dims = jnp.arange(head_size, dtype=jnp.int32)
    first_half = dims < head_size // 2
    freq_index = (dims % (head_size // 4)).astype(jnp.float32)
    rates = 3.0 * jnp.power(jnp.ones_like(freq_index) * 1.2, freq_index)
    coords = jnp.where(first_half[None, :], coord_one[:, None], coord_two[:, None])
    angles = coords * rates[None, :]
    return (jnp.cos(angles), jnp.sin(angles))


def rotate(tensor, cosine, sine_tab):
    row_count, head_count, head_size = tensor.shape
    quarters = tensor.reshape(row_count, head_count, 2, 2, head_size // 4)
    turned = jnp.stack([-quarters[:, :, :, 1], quarters[:, :, :, 0]], axis=3).reshape(tensor.shape)
    return tensor * cosine[:, None, :] + turned * sine_tab[:, None, :]


def softmax_rounded(scores):
    top = jnp.max(scores, axis=-1, keepdims=True)
    expo = jnp.exp(scores - top)
    return (expo / jnp.sum(expo, axis=-1, keepdims=True)).astype(jnp.bfloat16)


def merge_image(rows_all, side_len, offset):
    slot = jnp.arange(CAP, dtype=jnp.int32)
    half_side = side_len // 2
    across = slot // half_side
    along = slot % half_side
    valid = slot < half_side * half_side
    corner = jnp.arange(4, dtype=jnp.int32)
    source_rows = (
        offset
        + EXTRA
        + (2 * across[:, None] + corner[None, :] // 2) * side_len
        + 2 * along[:, None]
        + corner[None, :] % 2
    )
    source_rows = jnp.where(valid[:, None], source_rows, jnp.zeros_like(source_rows))
    picked = jnp.take(rows_all, source_rows, axis=0)
    return jnp.where(valid[:, None, None], picked, jnp.zeros_like(picked))


def dense_attention(queries, key_rows, value_rows, segment):
    group_rows = queries.shape[0]
    block_rows = 512

    def one_block(block_id):
        scores = jnp.einsum(
            "qhd,khd->hqk", queries, key_rows, preferred_element_type=jnp.float32
        ) / math.sqrt(HEAD)
        allowed = segment[None, :, None] == segment[None, None, :]
        scores = jnp.where(allowed, scores, jnp.full_like(scores, -1e30))
        weights = softmax_rounded(scores)
        return jnp.einsum(
            "hqk,khd->qhd", weights, value_rows, preferred_element_type=jnp.float32
        ).astype(jnp.bfloat16)

    stacked = lax.map(one_block, jnp.arange(group_rows // block_rows, dtype=jnp.int32))
    return stacked.reshape(queries.shape)


def body(stream_rows, ln_gain, ln_bias, w_q, w_k, w_v, w_o, scale_ls, sides, offsets, owners):
    fsdp_count = lax.axis_size("fsdp")
    group_rows = stream_rows.shape[0] * fsdp_count
    head_cols = w_q.shape[1]
    local_heads = head_cols // HEAD
    side_row = sides[0]
    offset_row = offsets[0]
    shard_rows = lax.all_gather(
        layer_norm(stream_rows, ln_gain, ln_bias), "fsdp", axis=0, tiled=True
    )
    projected = jnp.concatenate(
        [
            jnp.dot(shard_rows, w_q, preferred_element_type=jnp.float32),
            jnp.dot(shard_rows, w_k, preferred_element_type=jnp.float32),
            jnp.dot(shard_rows, w_v, preferred_element_type=jnp.float32),
        ],
        axis=1,
    )
    residual = lax.all_to_all(stream_rows, "fsdp", split_axis=1, concat_axis=0, tiled=True)
    segment, coord_one, coord_two = row_layout(side_row, offset_row, group_rows)
    cosine, sine_tab = rotary_tables(coord_one, coord_two, HEAD)
    queries = rotate(
        projected[:, :head_cols].reshape(group_rows, local_heads, HEAD), cosine, sine_tab
    ).astype(jnp.bfloat16)
    key_rows = rotate(
        projected[:, head_cols : 2 * head_cols].reshape(group_rows, local_heads, HEAD),
        cosine,
        sine_tab,
    ).astype(jnp.bfloat16)
    value_rows = (
        projected[:, 2 * head_cols :].astype(jnp.bfloat16).reshape(group_rows, local_heads, HEAD)
    )
    attended = dense_attention(queries, key_rows, value_rows, segment)
    partial_sum = jnp.dot(
        attended.reshape(group_rows, head_cols), w_o, preferred_element_type=jnp.float32
    )
    branch = lax.psum_scatter(
        partial_sum.astype(jnp.bfloat16), "fsdp", scatter_dimension=1, tiled=True
    ).astype(jnp.float32)
    updated = (residual.astype(jnp.float32) + scale_ls * branch).astype(jnp.bfloat16)

    def merge_entry(image_info):
        return merge_image(updated, image_info[0], image_info[1])

    merged = lax.map(merge_entry, (side_row, offset_row))
    group_id = lax.axis_index("dp")
    group_count = lax.axis_size("dp")
    targets = lax.dynamic_index_in_dim(owners, group_id, 0, keepdims=False)
    distance = (targets - group_id + group_count) % group_count
    carried = merged
    for level in range((group_count - 1).bit_length()):
        moved = shifted(carried, "dp", 1 << level)
        taken = distance // (1 << level) % 2 == 1
        carried = jnp.where(taken[:, None, None, None], moved, carried)
    return carried[None]


def solution(mesh):
    return jax.shard_map(
        body,
        mesh=mesh,
        in_specs=(
            P(("dp", "fsdp"), None),
            P(),
            P(),
            P(None, "fsdp"),
            P(None, "fsdp"),
            P(None, "fsdp"),
            P("fsdp", None),
            P("fsdp"),
            P("dp", None),
            P("dp", None),
            P(),
        ),
        out_specs=P("dp", None, None, None, "fsdp"),
        check_vma=False,
    )
```

profile of v0, /device:TPU:8, one launch (start us, length us, event | category | flops | bytes accessed | tf_op | source)
XLA Modules:
  0.0 330.2 jit_solution(13146252154444454191)
XLA Ops:
  6.5 0.0 copy-start
  6.5 0.0 all-gather.2.cloned.1.call-start
  6.5 1.4 convert_reduce_fusion
  7.9 1.3 fusion.4
  9.3 2.1 fusion.7
  11.4 0.0 all-gather.2.cloned.1.call-update
  11.4 0.0 reduce-scatter.2.cloned.1.call-start
  12.8 0.1 add_select_fusion.2
  13.0 0.2 broadcast_compare_fusion
  13.2 1.0 fusion.17
  14.2 106.2 %all-gather.2.cloned.1.call-done = bf16[512,4096]{1,0:T(8,128)(2,1)} async-done(((bf16[64,4096]{1,0:T(8,128)(2,1)}), bf16[512,4096]{1,0:T(8,128)(2,1)}) %all-gather.2.cloned.1.call-update) | async-done | bytes 4194320 | tf_op jit(solution)/shard_map/all_gather | solution.py:124
  120.4 0.0 copy-start.3
  120.4 0.0 copy-start.4
  120.4 4.3 %fusion.47 = f32[512,256]{0,1:T(8,128)S(1)} fusion(bf16[512,4096]{1,0:T(8,128)(2,1)} %all-gather.2.cloned.1.call-done, bf16[4096,256]{1,0:T(8,128)(2,1)} %param.14), kind=kOutput, calls=%fused_computation.99 | convolution fusion | flops 1073741824 | bytes 6815744 | tf_op jit(solution)/shard_map/dot_general | solution.py:129
  124.7 0.0 copy-done.3
  124.7 0.4 copy-done.4
  125.1 1.3 fusion.48
  126.5 0.1 pad_maximum_fusion
  126.6 0.3 fusion.13
  126.9 1.0 fusion.46
  127.9 4.2 %convolution_convert_fusion.2 = bf16[512,256]{0,1:T(8,128)(2,1)S(1)} fusion(bf16[512,4096]{1,0:T(8,128)(2,1)} %all-gather.2.cloned.1.call-done, bf16[4096,256]{1,0:T(8,128)(2,1)} %param.16), kind=kOutput, calls=%fused_computation.12 | convolution fusion | flops 1073872896 | bytes 6553600 | tf_op jit(solution)/shard_map/dot_general | solution.py:131
  132.1 1.3 convolution_convert_fusion.1
  133.3 0.0 copy-done
  133.4 3.2 convolution_convert_fusion
  136.6 0.0 copy-start.1
  136.6 0.0 reduce-scatter.2.cloned.1.call-update
  136.6 0.0 copy-start.2
  136.6 1.0 copy-done.1
  137.6 0.8 copy.27
  138.5 5.2 %all-to-all-start = ((bf16[64,8,512]{2,0,1:T(8,128)(2,1)}), bf16[64,8,512]{2,0,1:T(8,128)(2,1)S(1)}, u32[]{:S(2)}, u32[]{:S(2)}) async-start(bf16[64,8,512]{2,0,1:T(8,128)(2,1)} %bitcast.56), calls=%async_computation | async-start | bytes 1048576 | tf_op jit(solution)/shard_map/all_to_all | solution.py:135
  143.7 0.1 fusion.37
  143.8 0.1 compare_select_fusion
  143.9 0.1 reshape.606
  144.0 0.1 compare_and_fusion
  144.1 26.3 %all-to-all-done = bf16[64,8,512]{2,0,1:T(8,128)(2,1)S(1)} async-done(((bf16[64,8,512]{2,0,1:T(8,128)(2,1)}), bf16[64,8,512]{2,0,1:T(8,128)(2,1)S(1)}, u32[]{:S(2)}, u32[]{:S(2)}) %all-to-all-start) | async-done | bytes 524320 | tf_op jit(solution)/shard_map/all_to_all | solution.py:135
  170.4 91.1 %reduce-scatter.2.cloned.1.call-done = bf16[512,512]{1,0:T(8,128)(2,1)} async-done(((bf16[512,4096]{1,0:T(8,128)(2,1)}), bf16[512,512]{1,0:T(8,128)(2,1)}) %reduce-scatter.2.cloned.1.call-update) | async-done | bytes 524304 | tf_op jit(solution)/shard_map/reduce_scatter | solution.py:153
  261.5 0.0 copy-done.2
  261.5 1.2 fusion.8
  262.7 0.0 copy-start.5
  262.7 2.0 gather_fusion
  264.7 0.1 gather.8
  264.8 0.3 select_select_fusion
  265.1 0.3 collective-permute-start
  265.4 0.0 copy-done.5
  265.4 0.6 constant_dynamic-slice_fusion
  266.7 9.1 %collective-permute-done = bf16[1,81,4,512]{3,2,1,0:T(4,128)(2,1)S(1)} collective-permute-done((bf16[1,81,4,512]{3,2,1,0:T(4,128)(2,1)S(1)}, bf16[1,81,4,512]{3,2,1,0:T(4,128)(2,1)S(1)}, u32[]{:S(2)}, u32[]{:S(2)}) %collective-permute-start) | collective-permute-done | bytes 331808 | tf_op jit(solution)/shard_map/ppermute | solution.py:15
  275.9 0.4 broadcast_select_fusion
  276.2 0.1 collective-permute-start.1
  276.3 11.8 %collective-permute-done.1 = bf16[1,81,4,512]{3,2,1,0:T(4,128)(2,1)S(1)} collective-permute-done((bf16[1,81,4,512]{3,2,1,0:T(4,128)(2,1)S(1)}, bf16[1,81,4,512]{3,2,1,0:T(4,128)(2,1)S(1)}, u32[]{:S(2)}, u32[]{:S(2)}) %collective-permute-start.1) | collective-permute-done | bytes 331808 | tf_op jit(solution)/shard_map/ppermute | solution.py:15
  288.1 0.2 broadcast_select_fusion.1
  288.3 0.1 collective-permute-start.2
  288.4 13.1 %collective-permute-done.2 = bf16[1,81,4,512]{3,2,1,0:T(4,128)(2,1)S(1)} collective-permute-done((bf16[1,81,4,512]{3,2,1,0:T(4,128)(2,1)S(1)}, bf16[1,81,4,512]{3,2,1,0:T(4,128)(2,1)S(1)}, u32[]{:S(2)}, u32[]{:S(2)}) %collective-permute-start.2) | collective-permute-done | bytes 331808 | tf_op jit(solution)/shard_map/ppermute | solution.py:15
  301.5 0.2 broadcast_select_fusion.2
  301.7 0.1 collective-permute-start.3
  301.8 10.4 %collective-permute-done.3 = bf16[1,81,4,512]{3,2,1,0:T(4,128)(2,1)S(1)} collective-permute-done((bf16[1,81,4,512]{3,2,1,0:T(4,128)(2,1)S(1)}, bf16[1,81,4,512]{3,2,1,0:T(4,128)(2,1)S(1)}, u32[]{:S(2)}, u32[]{:S(2)}) %collective-permute-start.3) | collective-permute-done | bytes 331808 | tf_op jit(solution)/shard_map/ppermute | solution.py:15
  312.3 0.2 broadcast_select_fusion.3
  312.5 0.1 collective-permute-start.4
  312.6 9.9 %collective-permute-done.4 = bf16[1,81,4,512]{3,2,1,0:T(4,128)(2,1)S(1)} collective-permute-done((bf16[1,81,4,512]{3,2,1,0:T(4,128)(2,1)S(1)}, bf16[1,81,4,512]{3,2,1,0:T(4,128)(2,1)S(1)}, u32[]{:S(2)}, u32[]{:S(2)}) %collective-permute-start.4) | collective-permute-done | bytes 331808 | tf_op jit(solution)/shard_map/ppermute | solution.py:15
  322.5 0.9 select_bitcast_fusion
  (10 shorter events, 0.1 us)
Async XLA Ops:
  6.5 126.8 %copy-start = (bf16[256,4096]{1,0:T(8,128)(2,1)S(1)}, bf16[256,4096]{1,0:T(8,128)(2,1)}, u32[]{:S(2)}) copy-start(bf16[256,4096]{1,0:T(8,128)(2,1)} %param.17) | copy-start | bytes 6291460
  6.5 113.8 %all-gather.2.cloned.1.call-start = ((), (), s32[]{:S(2)}) async-start(), calls=%async_computation.2 | async-start | bytes 4718592 | tf_op jit(solution)/shard_map/all_gather | solution.py:124
  11.4 250.0 %reduce-scatter.2.cloned.1.call-start = ((), (), s32[]{:S(2)}) async-start(), calls=%async_computation.3 | async-start | bytes 4718592 | tf_op jit(solution)/shard_map/reduce_scatter | solution.py:153
  120.4 4.4 %copy-start.3 = (bf16[512,4096]{1,0:T(8,128)(2,1)S(1)}, bf16[512,4096]{1,0:T(8,128)(2,1)}, u32[]{:S(2)}) copy-start(bf16[512,4096]{1,0:T(8,128)(2,1)} %all-gather.2.cloned.1.call-done) | copy-start | bytes 12582916
  120.4 4.7 %copy-start.4 = (bf16[4096,256]{1,0:T(8,128)(2,1)S(1)}, bf16[4096,256]{1,0:T(8,128)(2,1)}, u32[]{:S(2)}) copy-start(bf16[4096,256]{1,0:T(8,128)(2,1)} %param.15) | copy-start | bytes 6291460
  136.6 1.0 copy-start.1
  136.6 124.9 %copy-start.2 = (f32[512]{0:T(512)S(1)}, f32[512]{0:T(512)}, u32[]{:S(2)}) copy-start(f32[512]{0:T(512)} %param.18) | copy-start | bytes 6148
  138.5 31.9 %all-to-all-start = ((bf16[64,8,512]{2,0,1:T(8,128)(2,1)}), bf16[64,8,512]{2,0,1:T(8,128)(2,1)S(1)}, u32[]{:S(2)}, u32[]{:S(2)}) async-start(bf16[64,8,512]{2,0,1:T(8,128)(2,1)} %bitcast.56), calls=%async_computation | async-start | bytes 1048576 | tf_op jit(solution)/shard_map/all_to_all | solution.py:135
  262.7 2.7 copy-start.5
  265.1 10.7 %collective-permute-start = (bf16[1,81,4,512]{3,2,1,0:T(4,128)(2,1)S(1)}, bf16[1,81,4,512]{3,2,1,0:T(4,128)(2,1)S(1)}, u32[]{:S(2)}, u32[]{:S(2)}) collective-permute-start(bf16[1,81,4,512]{3,2,1,0:T(4,128)(2,1)S(1)} %select_select_fusion), channel_id=1, source_target_pairs={{0,8},{8,16},{16,24},{24,32},{32,40},{40,48},{48,56},{56,64},{64,7... | collective-permute-start | bytes 995336 | tf_op jit(solution)/shard_map/ppermute | solution.py:15
  276.2 11.9 %collective-permute-start.1 = (bf16[1,81,4,512]{3,2,1,0:T(4,128)(2,1)S(1)}, bf16[1,81,4,512]{3,2,1,0:T(4,128)(2,1)S(1)}, u32[]{:S(2)}, u32[]{:S(2)}) collective-permute-start(bf16[1,81,4,512]{3,2,1,0:T(4,128)(2,1)S(1)} %broadcast_select_fusion), channel_id=1, source_target_pairs={{0,16},{8,24},{16,32},{24,40},{32,48},{40,56},{48,64},{56,72},{64,... | collective-permute-start | bytes 995336 | tf_op jit(solution)/shard_map/ppermute | solution.py:15
  288.3 13.2 %collective-permute-start.2 = (bf16[1,81,4,512]{3,2,1,0:T(4,128)(2,1)S(1)}, bf16[1,81,4,512]{3,2,1,0:T(4,128)(2,1)S(1)}, u32[]{:S(2)}, u32[]{:S(2)}) collective-permute-start(bf16[1,81,4,512]{3,2,1,0:T(4,128)(2,1)S(1)} %broadcast_select_fusion.1), channel_id=1, source_target_pairs={{0,32},{8,40},{16,48},{24,56},{32,64},{40,72},{48,80},{56,88},{64,... | collective-permute-start | bytes 995336 | tf_op jit(solution)/shard_map/ppermute | solution.py:15
  301.7 10.6 %collective-permute-start.3 = (bf16[1,81,4,512]{3,2,1,0:T(4,128)(2,1)S(1)}, bf16[1,81,4,512]{3,2,1,0:T(4,128)(2,1)S(1)}, u32[]{:S(2)}, u32[]{:S(2)}) collective-permute-start(bf16[1,81,4,512]{3,2,1,0:T(4,128)(2,1)S(1)} %broadcast_select_fusion.2), channel_id=1, source_target_pairs={{0,64},{8,72},{16,80},{24,88},{32,96},{40,104},{48,112},{56,120},{... | collective-permute-start | bytes 995336 | tf_op jit(solution)/shard_map/ppermute | solution.py:15
  312.5 10.0 %collective-permute-start.4 = (bf16[1,81,4,512]{3,2,1,0:T(4,128)(2,1)S(1)}, bf16[1,81,4,512]{3,2,1,0:T(4,128)(2,1)S(1)}, u32[]{:S(2)}, u32[]{:S(2)}) collective-permute-start(bf16[1,81,4,512]{3,2,1,0:T(4,128)(2,1)S(1)} %broadcast_select_fusion.3), channel_id=1, source_target_pairs={{0,128},{8,136},{16,144},{24,152},{32,160},{40,168},{48,176},{56,1... | collective-permute-start | bytes 995336 | tf_op jit(solution)/shard_map/ppermute | solution.py:15
Sparse Core Ops, SparseCore 0:
  11.6 108.7 all-gather.1
  136.7 124.7 reduce-scatter.1
where the time goes:
time: 331 us; the launch traced here: 330 us
  waiting for transfers between devices  278 us (84%)
  between operations  15.8 us (5%)
  matrix products  15.2 us (5%)
  other arithmetic  10.4 us (3%)
  starting transfers between devices  5.84 us (2%)
  local copies, waits for them, and re-layouts  5.13 us (2%)
    all_gather x1, waiting for transfers between devices, body(): lax.all_gather(layer_norm(stream_rows, ln_gain, ln_bias), 'fsdp', axis=0,...  106 us
    reduce_scatter x1, waiting for transfers between devices, body(): lax.psum_scatter(partial_sum.astype(jnp.bfloat16), 'fsdp', scatter_dimens...  91.1 us
    ppermute x5, waiting for transfers between devices, shifted(): lax.ppermute(array, axis, [(i, (i + by) % count) for i in range(count)])  54.3 us
    all_to_all x1, waiting for transfers between devices, body(): lax.all_to_all(stream_rows, 'fsdp', split_axis=1, concat_axis=0, tiled=True)  26.3 us
  transfers between devices with their start and end apart: 8, of which 8 were waited for; matrix products, arithmetic and copies ran while one was open for 1% of the time, Pallas kernels for 0%

commit v1 on v0

--- a/solution.py
+++ b/solution.py
@@ -3,6 +3,7 @@
 import jax.numpy as jnp
 from jax import lax
 from jax.sharding import PartitionSpec as P
+from jax.lax import all_to_all, axis_size
 
 HEAD = 128
 EXTRA = 5
@@ -121,9 +122,20 @@
     local_heads = head_cols // HEAD
     side_row = sides[0]
     offset_row = offsets[0]
-    shard_rows = lax.all_gather(
-        layer_norm(stream_rows, ln_gain, ln_bias), "fsdp", axis=0, tiled=True
-    )
+
+    def fix_series_all(mine_x, peer_axis):
+        new = jnp.concatenate(
+            all_to_all(
+                jnp.stack([mine_x] * axis_size(peer_axis), 0),
+                axis_name=peer_axis,
+                split_axis=0,
+                concat_axis=0,
+            ),
+            0,
+        )
+        return new
+
+    shard_rows = fix_series_all(layer_norm(stream_rows, ln_gain, ln_bias), "fsdp")
     projected = jnp.concatenate(
         [
             jnp.dot(shard_rows, w_q, preferred_element_type=jnp.float32),

time: 331 us -> 346 us (1.045)
  starting transfers between devices: 5.84 us -> 15.6 us
    all_gather x1 -> x0, waiting for transfers between devices: 106 us -> none  [body(): lax.all_gather(layer_norm(stream_rows, ln_gain, ln_bias), 'fsdp', axis=0,...]
    all_to_all x0 -> x1, waiting for transfers between devices: none -> 76.6 us  [fix_series_all(): all_to_all(jnp.stack([mine_x] * axis_size(peer_axis), 0), axis_name=peer_...]
    reduce_scatter x1, waiting for transfers between devices: 91.1 us -> 139 us  [body(): lax.psum_scatter(partial_sum.astype(jnp.bfloat16), 'fsdp', scatter_dimens...]
    all_to_all x1, waiting for transfers between devices: 26.3 us -> 9.86 us  [body(): lax.all_to_all(stream_rows, 'fsdp', split_axis=1, concat_axis=0, tiled=True)]
    all_to_all x0 -> x1, starting transfers between devices: none -> 11.5 us  [fix_series_all(): all_to_all(jnp.stack([mine_x] * axis_size(peer_axis), 0), axis_name=peer_...]
where the time goes in v1:
time: 346 us
  waiting for transfers between devices  280 us (81%)
  matrix products  17.6 us (5%)
  between operations  15.8 us (5%)
  starting transfers between devices  15.6 us (5%)
  other arithmetic  9.56 us (3%)
  local copies, waits for them, and re-layouts  7.27 us (2%)
    reduce_scatter x1, waiting for transfers between devices, body(): lax.psum_scatter(partial_sum.astype(jnp.bfloat16), 'fsdp', scatter_dimens...  139 us
    all_to_all x1, waiting for transfers between devices, fix_series_all(): all_to_all(jnp.stack([mine_x] * axis_size(peer_axis), 0), axis_name=peer_...  76.6 us
    ppermute x5, waiting for transfers between devices, shifted(): lax.ppermute(array, axis, [(i, (i + by) % count) for i in range(count)])  54.2 us
    all_to_all x1, starting transfers between devices, fix_series_all(): all_to_all(jnp.stack([mine_x] * axis_size(peer_axis), 0), axis_name=peer_...  11.5 us
    all_to_all x1, waiting for transfers between devices, body(): lax.all_to_all(stream_rows, 'fsdp', split_axis=1, concat_axis=0, tiled=True)  9.86 us
  transfers between devices with their start and end apart: 8, of which 8 were waited for; matrix products, arithmetic and copies ran while one was open for 1% of the time, Pallas kernels for 0%

profile of v1, /device:TPU:8, one launch (start us, length us, event | category | flops | bytes accessed | tf_op | source)
XLA Modules:
  0.0 345.7 jit_solution(14563132074367603790)
XLA Ops:
  6.5 0.0 copy-start
  6.5 1.4 convert_reduce_fusion
  7.9 1.3 fusion.4
  9.3 1.3 fusion.7
  10.6 2.5 stack.6
  13.1 11.5 %all-to-all-start.1 = ((bf16[8,64,4096]{2,1,0:T(8,128)(2,1)}), bf16[8,64,4096]{2,1,0:T(8,128)(2,1)}, u32[]{:S(2)}, u32[]{:S(2)}) async-start(bf16[8,64,4096]{2,1,0:T(8,128)(2,1)} %stack.6), calls=%async_computation.1 | async-start | bytes 8388608 | tf_op jit(solution)/shard_map/all_to_all | solution.py:128
  24.6 0.0 reduce-scatter.2.cloned.1.call-start
  26.0 0.1 add_select_fusion.2
  26.1 0.2 broadcast_compare_fusion
  26.4 1.0 fusion.17
  27.4 76.6 %all-to-all-done.1 = bf16[8,64,4096]{2,1,0:T(8,128)(2,1)} async-done(((bf16[8,64,4096]{2,1,0:T(8,128)(2,1)}), bf16[8,64,4096]{2,1,0:T(8,128)(2,1)}, u32[]{:S(2)}, u32[]{:S(2)}) %all-to-all-start.1) | async-done | bytes 4194336 | tf_op jit(solution)/shard_map/all_to_all | solution.py:128
  104.0 0.0 copy-start.3
  104.0 5.0 %convolution_convert_fusion.2 = bf16[512,256]{0,1:T(8,128)(2,1)} fusion(bf16[512,4096]{1,0:T(8,128)(2,1)} %bitcast.11, bf16[4096,256]{1,0:T(8,128)(2,1)} %param.16), kind=kOutput, calls=%fused_computation.12 | convolution fusion | flops 1073872896 | bytes 6553600 | tf_op jit(solution)/shard_map/dot_general | solution.py:143
  109.0 0.0 copy-done.3
  109.0 0.0 copy-start.4
  109.0 3.6 %fusion.47 = f32[512,256]{0,1:T(8,128)S(1)} fusion(bf16[512,4096]{1,0:T(8,128)(2,1)} %bitcast.11, bf16[4096,256]{1,0:T(8,128)(2,1)S(1)} %copy-done.3), kind=kOutput, calls=%fused_computation.99 | convolution fusion | flops 1073741824 | bytes 6815744 | tf_op jit(solution)/shard_map/dot_general | solution.py:141
  112.7 0.0 copy-done.4
  112.7 3.5 %fusion.48 = f32[512,256]{0,1:T(8,128)S(1)} fusion(bf16[512,4096]{1,0:T(8,128)(2,1)} %bitcast.11, bf16[4096,256]{1,0:T(8,128)(2,1)S(1)} %copy-done.4), kind=kOutput, calls=%fused_computation.100 | convolution fusion | flops 1073741824 | bytes 6815744 | tf_op jit(solution)/shard_map/dot_general | solution.py:142
  116.3 0.1 pad_maximum_fusion
  116.4 0.3 fusion.13
  116.7 0.0 copy-start.6
  116.7 1.0 fusion.46
  117.7 0.0 copy-done.6
  117.7 1.3 convolution_convert_fusion.1
  119.0 0.0 copy-done
  119.0 3.2 convolution_convert_fusion
  122.2 0.0 copy-start.1
  122.2 0.0 reduce-scatter.2.cloned.1.call-update
  122.2 0.0 copy-start.2
  122.3 1.0 copy-done.1
  123.3 0.8 copy.27
  124.1 3.6 %all-to-all-start = ((bf16[64,8,512]{2,0,1:T(8,128)(2,1)}), bf16[64,8,512]{2,0,1:T(8,128)(2,1)S(1)}, u32[]{:S(2)}, u32[]{:S(2)}) async-start(bf16[64,8,512]{2,0,1:T(8,128)(2,1)} %bitcast.57), calls=%async_computation | async-start | bytes 1048576 | tf_op jit(solution)/shard_map/all_to_all | solution.py:147
  127.8 0.1 fusion.37
  127.9 0.1 compare_select_fusion
  128.0 0.1 reshape.612
  128.2 0.1 compare_and_fusion
  128.3 9.9 %all-to-all-done = bf16[64,8,512]{2,0,1:T(8,128)(2,1)S(1)} async-done(((bf16[64,8,512]{2,0,1:T(8,128)(2,1)}), bf16[64,8,512]{2,0,1:T(8,128)(2,1)S(1)}, u32[]{:S(2)}, u32[]{:S(2)}) %all-to-all-start) | async-done | bytes 524320 | tf_op jit(solution)/shard_map/all_to_all | solution.py:147
  138.1 139.1 %reduce-scatter.2.cloned.1.call-done = bf16[512,512]{1,0:T(8,128)(2,1)} async-done(((bf16[512,4096]{1,0:T(8,128)(2,1)}), bf16[512,512]{1,0:T(8,128)(2,1)}) %reduce-scatter.2.cloned.1.call-update) | async-done | bytes 524304 | tf_op jit(solution)/shard_map/reduce_scatter | solution.py:165
  277.3 0.0 copy-done.2
  277.3 1.2 fusion.8
  278.5 0.0 copy-start.5
  278.5 2.0 gather_fusion
  280.5 0.1 gather.8
  280.6 0.3 select_select_fusion
  280.9 0.1 collective-permute-start
  281.0 0.0 copy-done.5
  281.0 0.6 constant_dynamic-slice_fusion
  282.3 9.1 %collective-permute-done = bf16[1,81,4,512]{3,2,1,0:T(4,128)(2,1)S(1)} collective-permute-done((bf16[1,81,4,512]{3,2,1,0:T(4,128)(2,1)S(1)}, bf16[1,81,4,512]{3,2,1,0:T(4,128)(2,1)S(1)}, u32[]{:S(2)}, u32[]{:S(2)}) %collective-permute-start) | collective-permute-done | bytes 331808 | tf_op jit(solution)/shard_map/ppermute | solution.py:16
  291.5 0.4 broadcast_select_fusion
  291.8 0.1 collective-permute-start.1
  292.0 11.9 %collective-permute-done.1 = bf16[1,81,4,512]{3,2,1,0:T(4,128)(2,1)S(1)} collective-permute-done((bf16[1,81,4,512]{3,2,1,0:T(4,128)(2,1)S(1)}, bf16[1,81,4,512]{3,2,1,0:T(4,128)(2,1)S(1)}, u32[]{:S(2)}, u32[]{:S(2)}) %collective-permute-start.1) | collective-permute-done | bytes 331808 | tf_op jit(solution)/shard_map/ppermute | solution.py:16
  303.8 0.2 broadcast_select_fusion.1
  304.0 0.1 collective-permute-start.2
  304.1 13.0 %collective-permute-done.2 = bf16[1,81,4,512]{3,2,1,0:T(4,128)(2,1)S(1)} collective-permute-done((bf16[1,81,4,512]{3,2,1,0:T(4,128)(2,1)S(1)}, bf16[1,81,4,512]{3,2,1,0:T(4,128)(2,1)S(1)}, u32[]{:S(2)}, u32[]{:S(2)}) %collective-permute-start.2) | collective-permute-done | bytes 331808 | tf_op jit(solution)/shard_map/ppermute | solution.py:16
  317.2 0.2 broadcast_select_fusion.2
  317.3 0.1 collective-permute-start.3
  317.5 10.4 %collective-permute-done.3 = bf16[1,81,4,512]{3,2,1,0:T(4,128)(2,1)S(1)} collective-permute-done((bf16[1,81,4,512]{3,2,1,0:T(4,128)(2,1)S(1)}, bf16[1,81,4,512]{3,2,1,0:T(4,128)(2,1)S(1)}, u32[]{:S(2)}, u32[]{:S(2)}) %collective-permute-start.3) | collective-permute-done | bytes 331808 | tf_op jit(solution)/shard_map/ppermute | solution.py:16
  327.8 0.2 broadcast_select_fusion.3
  328.0 0.1 collective-permute-start.4
  328.1 9.8 %collective-permute-done.4 = bf16[1,81,4,512]{3,2,1,0:T(4,128)(2,1)S(1)} collective-permute-done((bf16[1,81,4,512]{3,2,1,0:T(4,128)(2,1)S(1)}, bf16[1,81,4,512]{3,2,1,0:T(4,128)(2,1)S(1)}, u32[]{:S(2)}, u32[]{:S(2)}) %collective-permute-start.4) | collective-permute-done | bytes 331808 | tf_op jit(solution)/shard_map/ppermute | solution.py:16
  337.9 0.9 select_bitcast_fusion
  (10 shorter events, 0.1 us)
Async XLA Ops:
  6.5 112.4 %copy-start = (bf16[256,4096]{1,0:T(8,128)(2,1)S(1)}, bf16[256,4096]{1,0:T(8,128)(2,1)}, u32[]{:S(2)}) copy-start(bf16[256,4096]{1,0:T(8,128)(2,1)} %param.17) | copy-start | bytes 6291460
  13.1 90.9 %all-to-all-start.1 = ((bf16[8,64,4096]{2,1,0:T(8,128)(2,1)}), bf16[8,64,4096]{2,1,0:T(8,128)(2,1)}, u32[]{:S(2)}, u32[]{:S(2)}) async-start(bf16[8,64,4096]{2,1,0:T(8,128)(2,1)} %stack.6), calls=%async_computation.1 | async-start | bytes 8388608 | tf_op jit(solution)/shard_map/all_to_all | solution.py:128
  24.6 252.6 %reduce-scatter.2.cloned.1.call-start = ((), (), s32[]{:S(2)}) async-start(), calls=%async_computation.3 | async-start | bytes 4718592 | tf_op jit(solution)/shard_map/reduce_scatter | solution.py:165
  104.0 5.0 %copy-start.3 = (bf16[4096,256]{1,0:T(8,128)(2,1)S(1)}, bf16[4096,256]{1,0:T(8,128)(2,1)}, u32[]{:S(2)}) copy-start(bf16[4096,256]{1,0:T(8,128)(2,1)} %param.14) | copy-start | bytes 6291460
  109.0 3.7 %copy-start.4 = (bf16[4096,256]{1,0:T(8,128)(2,1)S(1)}, bf16[4096,256]{1,0:T(8,128)(2,1)}, u32[]{:S(2)}) copy-start(bf16[4096,256]{1,0:T(8,128)(2,1)} %param.15) | copy-start | bytes 6291460
  116.7 1.0 copy-start.6
  122.2 1.0 copy-start.1
  122.2 155.0 %copy-start.2 = (f32[512]{0:T(512)S(1)}, f32[512]{0:T(512)}, u32[]{:S(2)}) copy-start(f32[512]{0:T(512)} %param.18) | copy-start | bytes 6148
  124.1 14.0 %all-to-all-start = ((bf16[64,8,512]{2,0,1:T(8,128)(2,1)}), bf16[64,8,512]{2,0,1:T(8,128)(2,1)S(1)}, u32[]{:S(2)}, u32[]{:S(2)}) async-start(bf16[64,8,512]{2,0,1:T(8,128)(2,1)} %bitcast.57), calls=%async_computation | async-start | bytes 1048576 | tf_op jit(solution)/shard_map/all_to_all | solution.py:147
  278.5 2.6 copy-start.5
  280.9 10.5 %collective-permute-start = (bf16[1,81,4,512]{3,2,1,0:T(4,128)(2,1)S(1)}, bf16[1,81,4,512]{3,2,1,0:T(4,128)(2,1)S(1)}, u32[]{:S(2)}, u32[]{:S(2)}) collective-permute-start(bf16[1,81,4,512]{3,2,1,0:T(4,128)(2,1)S(1)} %select_select_fusion), channel_id=1, source_target_pairs={{0,8},{8,16},{16,24},{24,32},{32,40},{40,48},{48,56},{56,64},{64,7... | collective-permute-start | bytes 995336 | tf_op jit(solution)/shard_map/ppermute | solution.py:16
  291.8 12.0 %collective-permute-start.1 = (bf16[1,81,4,512]{3,2,1,0:T(4,128)(2,1)S(1)}, bf16[1,81,4,512]{3,2,1,0:T(4,128)(2,1)S(1)}, u32[]{:S(2)}, u32[]{:S(2)}) collective-permute-start(bf16[1,81,4,512]{3,2,1,0:T(4,128)(2,1)S(1)} %broadcast_select_fusion), channel_id=1, source_target_pairs={{0,16},{8,24},{16,32},{24,40},{32,48},{40,56},{48,64},{56,72},{64,... | collective-permute-start | bytes 995336 | tf_op jit(solution)/shard_map/ppermute | solution.py:16
  304.0 13.1 %collective-permute-start.2 = (bf16[1,81,4,512]{3,2,1,0:T(4,128)(2,1)S(1)}, bf16[1,81,4,512]{3,2,1,0:T(4,128)(2,1)S(1)}, u32[]{:S(2)}, u32[]{:S(2)}) collective-permute-start(bf16[1,81,4,512]{3,2,1,0:T(4,128)(2,1)S(1)} %broadcast_select_fusion.1), channel_id=1, source_target_pairs={{0,32},{8,40},{16,48},{24,56},{32,64},{40,72},{48,80},{56,88},{64,... | collective-permute-start | bytes 995336 | tf_op jit(solution)/shard_map/ppermute | solution.py:16
  317.3 10.5 %collective-permute-start.3 = (bf16[1,81,4,512]{3,2,1,0:T(4,128)(2,1)S(1)}, bf16[1,81,4,512]{3,2,1,0:T(4,128)(2,1)S(1)}, u32[]{:S(2)}, u32[]{:S(2)}) collective-permute-start(bf16[1,81,4,512]{3,2,1,0:T(4,128)(2,1)S(1)} %broadcast_select_fusion.2), channel_id=1, source_target_pairs={{0,64},{8,72},{16,80},{24,88},{32,96},{40,104},{48,112},{56,120},{... | collective-permute-start | bytes 995336 | tf_op jit(solution)/shard_map/ppermute | solution.py:16
  328.0 9.9 %collective-permute-start.4 = (bf16[1,81,4,512]{3,2,1,0:T(4,128)(2,1)S(1)}, bf16[1,81,4,512]{3,2,1,0:T(4,128)(2,1)S(1)}, u32[]{:S(2)}, u32[]{:S(2)}) collective-permute-start(bf16[1,81,4,512]{3,2,1,0:T(4,128)(2,1)S(1)} %broadcast_select_fusion.3), channel_id=1, source_target_pairs={{0,128},{8,136},{16,144},{24,152},{32,160},{40,168},{48,176},{56,1... | collective-permute-start | bytes 995336 | tf_op jit(solution)/shard_map/ppermute | solution.py:16
Sparse Core Ops, SparseCore 0:
  122.4 154.8 reduce-scatter.1
